TPU v7x, 256 devices: a whole 4x4x8 slice. The times are simulated.
256 devices in a mesh: var: 8 (over y, core), tok: 32 (over x, z).
Axes of the slice: x: 4, y: 4, z: 8, core: 2. Of those that a mesh axis runs over, the one named last changes fastest.
Arguments:
- patches: bfloat16 [72, 4, 4096], P('var', None, 'tok'), may hold values from -6 to 6
- slot_var: int32 [72], replicated, may hold values from -1 to 47, as said below
- patch_weight: bfloat16 [48, 4, 1024], replicated, may hold values from -3 to 3
- var_embed: bfloat16 [48, 1024], replicated, may hold values from -6 to 6
- query: bfloat16 [1024], replicated, may hold values from -16 to 16
- key_weight: bfloat16 [1024, 1024], P('tok'), may hold values from -0.1875 to 0.1875
- value_weight: bfloat16 [1024, 1024], P('tok'), may hold values from -0.1875 to 0.1875
- out_weight: bfloat16 [1024, 1024], P('tok'), may hold values from -0.1875 to 0.1875
- cotangent: bfloat16 [4096, 1024], P(('tok', 'var')), may hold values from -6 to 6
Outputs:
- aggregated: bfloat16 [4096, 1024], P(('tok', 'var'))
- patch_grad: float32 [72, 4096], P('var', 'tok')
Inputs may be any that keep to these rules, and one draw needn't show every extreme that they name: `slot_var`: slot 9 * i + j belongs to index i of var. Every variable id stands in exactly one slot; empty slots hold -1. The live slots of an index come first and hold consecutive ids, rising from index to index. Every index holds at least one and at most 9 live slots, and some index holds exactly 9.
All inputs are finite; a program needn't handle non-finite values.
Results may differ from a plain program's by a relative error of at most 0.011.
Values may be sent and summed in bfloat16 or wider, within the bound.
No kernel may reach another device: no remote copies, remote signals or barrier semaphores. Data moves between devices by JAX's collectives and lax.ppermute only.
A program may use at most 128 MiB of HBM per device.

v0:
```python
import math
import jax
import jax.numpy as jnp
from jax import lax
from jax.sharding import PartitionSpec as P

H = 16
HD = 64
score_cap = 5.0
inv_sqrt_two = 1.0 / math.sqrt(2.0)
inv_sqrt_two_pi = 1.0 / math.sqrt(2.0 * math.pi)
f32 = jnp.float32
bf16 = jnp.bfloat16


def gelu_exact(inputs):
    return 0.5 * inputs * (1.0 + lax.erf(inputs * inv_sqrt_two))


def gelu_slope(inputs):
    return (
        0.5 * (1.0 + lax.erf(inputs * inv_sqrt_two))
        + inputs * jnp.exp(-0.5 * inputs * inputs) * inv_sqrt_two_pi
    )


def live_index(slot_var, var_total):
    ids = jnp.arange(var_total, dtype=jnp.int32)
    places = jnp.arange(slot_var.shape[0], dtype=jnp.int32)
    match = slot_var[None, :] == ids[:, None]
    return jnp.sum(jnp.where(match, places[None, :], 0), axis=1)


def split(x):
    hi = x.astype(bf16)
    lo = (x - hi.astype(f32)).astype(bf16)
    return (hi, lo)


def ein(spec, a, b):
    return jnp.einsum(spec, a, b, preferred_element_type=f32)


def ring_steps(block, n, perm_of):
    forward, backward = (block, block)
    behind, ahead = ([], [])
    for k in range(1, n // 2 + 1):
        forward = lax.ppermute(forward, "tok", perm_of(1))
        behind.append(forward)
        if k < n - k:
            backward = lax.ppermute(backward, "tok", perm_of(-1))
            ahead.append(backward)
    return jnp.stack([block] + behind + ahead[::-1])


def ring_gather(block, n_x, n_z):

    def along_z(step):
        return [(x * n_z + z, x * n_z + (z + step) % n_z) for x in range(n_x) for z in range(n_z)]

    def along_x(step):
        return [(x * n_z + z, (x + step) % n_x * n_z + z) for x in range(n_x) for z in range(n_z)]

    me = lax.axis_index("tok")
    my_z, my_x = (me % n_z, me // n_z)
    by_z = ring_steps(block, n_z, along_z)
    by_z = jnp.take(by_z, (my_z - jnp.arange(n_z)) % n_z, axis=0)
    by_x = ring_steps(by_z, n_x, along_x)
    by_x = jnp.take(by_x, (my_x - jnp.arange(n_x)) % n_x, axis=0)
    return by_x.reshape((n_x * n_z * block.shape[0],) + block.shape[1:])


def body(
    patches,
    slot_var,
    patch_weight,
    var_embed,
    query,
    key_weight,
    value_weight,
    out_weight,
    cotangent,
    *,
    n_var,
    n_tok,
    n_tok_x,
    n_tok_z
):
    var_total, pixels_per, width = patch_weight.shape
    local_slots = patches.shape[0]
    rows = key_weight.shape[0]
    tok_count = cotangent.shape[0]
    query_heads = query.reshape(H, HD).astype(f32)
    wq_rows = jnp.sum(key_weight.reshape(rows, H, HD).astype(f32) * query_heads[None], axis=2)
    wq_copies = jnp.broadcast_to(wq_rows[None], (n_tok, rows, H))
    wq_full = lax.all_to_all(wq_copies, "tok", 0, 0, tiled=True).reshape(n_tok * rows, H)
    wq_hi, wq_lo = split(wq_full)
    core = lax.axis_index("var") % 2
    mine = jnp.where(core == 0, value_weight, out_weight)
    gathered = ring_gather(mine, n_tok_x, n_tok_z)
    other = lax.ppermute(gathered, "var", [(i, i ^ 1) for i in range(n_var)])
    value_matrix = jnp.where(core == 0, gathered, other)
    out_matrix = jnp.where(core == 0, other, gathered)
    slot_pixels = lax.all_to_all(patches, "var", 2, 0, tiled=True)
    live_slot = live_index(slot_var, var_total)
    pixels = jnp.take(slot_pixels, live_slot, axis=0)
    pre_act = ein("vpt,vpd->vtd", pixels, patch_weight) + var_embed.astype(f32)[:, None, :]
    embedded = gelu_exact(pre_act).astype(bf16)
    slope = lax.optimization_barrier(gelu_slope(pre_act))
    raw_scores = (
        ein("vtd,dh->tvh", embedded, wq_hi) + ein("vtd,dh->tvh", embedded, wq_lo)
    ) / math.sqrt(HD)
    squashed = jnp.tanh(raw_scores / score_cap)
    exp_scores = jnp.exp(score_cap * squashed)
    attn_f32 = exp_scores / jnp.sum(exp_scores, axis=1, keepdims=True)
    attn_bf = attn_f32.astype(bf16)
    same_head = jnp.arange(H)[:, None] == jnp.arange(H)[None, :]
    mixed_in = ein("tvh,vtd->thd", attn_bf, embedded)
    mix_hi, mix_lo = split(mixed_in)
    rows_both = jnp.concatenate([mix_hi, mix_lo], axis=0).reshape(2 * tok_count * H, width)
    all_heads = jnp.dot(rows_both, value_matrix, preferred_element_type=f32).reshape(
        2, tok_count, H, H, HD
    )
    pooled = (
        jnp.sum(jnp.where(same_head[None, None, :, :, None], all_heads, 0.0), axis=(0, 3))
        .astype(bf16)
        .reshape(tok_count, width)
    )
    mixed_out = jnp.dot(pooled, out_matrix, preferred_element_type=f32).astype(bf16)
    cot_t = lax.optimization_barrier(cotangent.T)
    grad_pooled = (
        jnp.dot(out_matrix, cot_t, preferred_element_type=f32)
        .T.astype(bf16)
        .reshape(tok_count, H, HD)
    )
    by_head = jnp.where(
        same_head[:, None, None, :], grad_pooled.transpose(1, 2, 0)[:, :, :, None], 0
    )
    spread_t = jnp.dot(
        value_matrix, by_head.reshape(width, tok_count * H).astype(bf16), preferred_element_type=f32
    )
    spread = spread_t.reshape(width, tok_count, H).transpose(1, 2, 0)
    spread_hi, spread_lo = split(spread)
    both = ein("vtd,thd->tvh", embedded, jnp.concatenate([spread_hi, spread_lo], axis=1))
    grad_attn = both[:, :, :H] + both[:, :, H:]
    grad_scores = attn_f32 * (grad_attn - jnp.sum(attn_f32 * grad_attn, axis=1, keepdims=True))
    grad_raw = grad_scores * (1.0 - squashed * squashed) / math.sqrt(HD)
    raw_hi, raw_lo = split(grad_raw)
    left = jnp.concatenate([attn_bf, attn_bf, raw_hi, raw_hi, raw_lo], axis=2)
    wq_t = jnp.concatenate([wq_hi.T, wq_lo.T, wq_hi.T], axis=0)
    right = jnp.concatenate(
        [spread_hi, spread_lo, jnp.broadcast_to(wq_t[None], (tok_count,) + wq_t.shape)], axis=1
    )
    grad_embed = ein("tvk,tkd->vtd", left, right).astype(bf16)
    grad_pre = grad_embed.astype(f32) * slope
    partial = jnp.einsum(
        "vpt,vtd->vpd", pixels.astype(f32), grad_pre, precision=lax.Precision.HIGHEST
    ).reshape(var_total, pixels_per * width)
    slots = n_var * local_slots
    cols = partial.shape[1] // n_tok
    safe = jnp.clip(slot_var, 0, var_total - 1)
    slot_rows = jnp.where((slot_var >= 0)[:, None], jnp.take(partial, safe, axis=0), 0.0)
    blocks = slot_rows.reshape(n_var, local_slots, n_tok, cols)
    by_var = lax.all_to_all(blocks, "var", 0, 0, tiled=True).sum(axis=0)
    by_tok = lax.all_to_all(by_var.transpose(1, 0, 2), "tok", 0, 0, tiled=True).sum(axis=0)
    del slots
    return (mixed_out, by_tok)


def inner_ring(mesh, n_tok):
    try:
        row = mesh.devices[0]
        slow = [tuple(d.coords)[0] for d in row]
        size = next((i for i in range(1, n_tok) if slow[i] != slow[0]), n_tok)
        if n_tok % size == 0:
            return size
    except (AttributeError, TypeError, IndexError):
        pass
    return n_tok


def solution(mesh):
    import functools

    n_tok = mesh.shape["tok"]
    n_tok_z = inner_ring(mesh, n_tok)
    fn = functools.partial(
        body, n_var=mesh.shape["var"], n_tok=n_tok, n_tok_x=n_tok // n_tok_z, n_tok_z=n_tok_z
    )
    return jax.shard_map(
        fn,
        mesh=mesh,
        in_specs=(
            P("var", None, "tok"),
            P(),
            P(),
            P(),
            P(),
            P("tok", None),
            P("tok", None),
            P("tok", None),
            P(("tok", "var"), None),
        ),
        out_specs=(P(("tok", "var"), None), P("var", "tok")),
        check_vma=False,
    )
```

profile of v0, /device:TPU:32, one launch (start us, length us, event | category | flops | bytes accessed | tf_op | source)
XLA Modules:
  0.0 157.5 jit_solution(6378815027409704544)
XLA Ops:
  5.3 4.5 %all-to-all-start.1 = ((bf16[8,2,288]{2,1,0:T(2,128)(2,1)}), bf16[8,2,288]{2,1,0:T(2,128)(2,1)S(1)}, u32[]{:S(2)}, u32[]{:S(2)}) async-start(bf16[8,2,288]{2,1,0:T(2,128)(2,1)} %reshape.267), calls=%async_computation.1 | async-start | bytes 24576 | tf_op jit(solution)/shard_map/all_to_all | solution.py:104
  14.6 2.2 %collective-permute-start.5 = (bf16[32,1024]{1,0:T(8,128)(2,1)S(1)}, bf16[32,1024]{1,0:T(8,128)(2,1)S(1)}, u32[]{:S(2)}, u32[]{:S(2)}) collective-permute-start(bf16[32,1024]{1,0:T(8,128)(2,1)S(1)} %collective-permute-done.4), channel_id=1, source_target_pairs={{0,7},{1,0},{2,1},{3,2},{4,3},{5,4},{6,5},{7,6},{8,15},{9,8},{10,9... | collective-permute-start | bytes 196616 | tf_op jit(solution)/shard_map/ppermute | solution.py:51
  16.8 2.6 %collective-permute-done.1 = bf16[32,1024]{1,0:T(8,128)(2,1)S(1)} collective-permute-done((bf16[32,1024]{1,0:T(8,128)(2,1)S(1)}, bf16[32,1024]{1,0:T(8,128)(2,1)S(1)}, u32[]{:S(2)}, u32[]{:S(2)}) %collective-permute-start.1) | collective-permute-done | bytes 65568 | tf_op jit(solution)/shard_map/ppermute | solution.py:48
  20.2 2.3 %collective-permute-start.6 = (bf16[32,1024]{1,0:T(8,128)(2,1)S(1)}, bf16[32,1024]{1,0:T(8,128)(2,1)S(1)}, u32[]{:S(2)}, u32[]{:S(2)}) collective-permute-start(bf16[32,1024]{1,0:T(8,128)(2,1)S(1)} %collective-permute-done.5), channel_id=1, source_target_pairs={{0,7},{1,0},{2,1},{3,2},{4,3},{5,4},{6,5},{7,6},{8,15},{9,8},{10,9... | collective-permute-start | bytes 196616 | tf_op jit(solution)/shard_map/ppermute | solution.py:51
  24.8 5.4 %collective-permute-done.3 = bf16[32,1024]{1,0:T(8,128)(2,1)S(1)} collective-permute-done((bf16[32,1024]{1,0:T(8,128)(2,1)S(1)}, bf16[32,1024]{1,0:T(8,128)(2,1)S(1)}, u32[]{:S(2)}, u32[]{:S(2)}) %collective-permute-start.3) | collective-permute-done | bytes 65568 | tf_op jit(solution)/shard_map/ppermute | solution.py:48
  34.3 9.3 %collective-permute-done.7 = bf16[8,32,1024]{2,1,0:T(8,128)(2,1)S(1)} collective-permute-done((bf16[8,32,1024]{2,1,0:T(8,128)(2,1)S(1)}, bf16[8,32,1024]{2,1,0:T(8,128)(2,1)S(1)}, u32[]{:S(2)}, u32[]{:S(2)}) %collective-permute-start.7) | collective-permute-done | bytes 524320 | tf_op jit(solution)/shard_map/ppermute | solution.py:48
  44.9 10.5 %collective-permute-done.8 = bf16[8,32,1024]{2,1,0:T(8,128)(2,1)S(1)} collective-permute-done((bf16[8,32,1024]{2,1,0:T(8,128)(2,1)S(1)}, bf16[8,32,1024]{2,1,0:T(8,128)(2,1)S(1)}, u32[]{:S(2)}, u32[]{:S(2)}) %collective-permute-start.8) | collective-permute-done | bytes 524320 | tf_op jit(solution)/shard_map/ppermute | solution.py:48
  57.0 2.3 %gather_fusion.2 = bf16[4,8,32,1024]{3,2,1,0:T(8,128)(2,1)S(1)} fusion(bf16[4,8,32,1024]{3,2,1,0:T(8,128)(2,1)} %pad_maximum_fusion, s32[1024]{0:T(1024)S(1)} %pad_clamp_fusion.1), kind=kCustom, calls=%fused_computation.2 | custom fusion | bytes 4194320 | tf_op jit(solution)/shard_map/jit(_take)/gather | solution.py:69
  63.8 9.5 %all-to-all-start = ((f32[32,1,512]{2,1,0:T(1,128)}), f32[32,1,512]{2,1,0:T(1,128)S(1)}, u32[]{:S(2)}, u32[]{:S(2)}) async-start(f32[32,1,512]{2,1,0:T(1,128)} %reshape.269), calls=%async_computation | async-start | bytes 131072 | tf_op jit(solution)/shard_map/all_to_all | solution.py:96
  74.7 3.8 %fusion.4 = (f32[48,16,1024]{2,1,0:T(8,128)}, bf16[48,16,1024]{2,1,0:T(8,128)(2,1)}) fusion(f32[48,1024]{1,0:T(8,128)S(1)} %convert_element_type.95, bf16[48,4,1024]{2,1,0:T(4,128)(2,1)S(1)} %copy-done, bf16[48,4,16]{2,1,0:T(4,128)(2,1)S(1)} %gather_fusion, pred[48]{0:T(512)(128)(4,1)S(1)} %compare_and_fusion.3), kind=kOutput, calls=%fused_computation.10 | convolution fusion | flops 15731712 | bytes 5314608 | tf_op jit(solution)/shard_map/vpt,vpd->vtd/dot_general | solution.py:41
  78.5 4.0 %all-to-all-done = f32[32,1,512]{2,1,0:T(1,128)S(1)} async-done(((f32[32,1,512]{2,1,0:T(1,128)}), f32[32,1,512]{2,1,0:T(1,128)S(1)}, u32[]{:S(2)}, u32[]{:S(2)}) %all-to-all-start) | async-done | bytes 65568 | tf_op jit(solution)/shard_map/all_to_all | solution.py:96
  84.2 2.5 %fusion.30 = f32[16,48,16]{1,0,2:T(8,128)S(1)} fusion(bf16[48,16,1024]{2,1,0:T(8,128)(2,1)} %get-tuple-element.13, f32[1024,16]{0,1:T(8,128)S(1)} %reshape.224), kind=kOutput, calls=%fused_computation.52 | convolution fusion | flops 25182208 | bytes 1687552 | tf_op jit(solution)/shard_map/vtd,dh->tvh/dot_general | solution.py:41
  86.7 2.5 %bitcast_reduce_fusion = (f32[16,16]{1,0:T(8,128)S(1)}, f32[16,48,16]{1,0,2:T(8,128)S(1)}) fusion(f32[16,48,16]{1,0,2:T(8,128)S(1)} %fusion.30, bf16[48,16,1024]{2,1,0:T(8,128)(2,1)} %get-tuple-element.13, f32[1024,16]{0,1:T(8,128)S(1)} %reshape.224), kind=kOutput, calls=%fused_computation.60 | convolution fusion | flops 25280256 | bytes 1737728 | tf_op jit(solution)/shard_map/vtd,dh->tvh/dot_general | solution.py:41
  90.7 2.8 %subtract_convert_fusion.1 = (bf16[16,16,1024]{2,1,0:T(8,128)(2,1)}, bf16[16,16,1024]{2,1,0:T(8,128)(2,1)}) fusion(bf16[16,48,16]{1,2,0:T(8,128)(2,1)S(1)} %get-tuple-element.7, bf16[48,16,1024]{2,1,0:T(8,128)(2,1)S(1)} %copy-done.1), kind=kOutput, calls=%fused_computation.46 | convolution fusion | flops 26214400 | bytes 2646016 | tf_op jit(solution)/shard_map/tvh,vtd->thd/dot_general | solution.py:41
  93.5 2.2 %fusion.21 = bf16[16,1024]{1,0:T(8,128)(2,1)S(1)} fusion(bf16[1024,16]{0,1:T(8,128)(2,1)S(1)} %bitcast.137, bf16[1024,1024]{1,0:T(8,128)(2,1)} %collective-permute-done.10, bf16[1024,1024]{1,0:T(8,128)(2,1)} %bitcast_select_fusion, pred[]{:T(512)S(6)} %eq.58), kind=kOutput, calls=%fused_computation.39 | convolution fusion | flops 34619392 | bytes 4259841 | tf_op jit(solution)/shard_map/dot_general | solution.py:132
  99.1 2.6 %subtract_convert_fusion = (bf16[16,16,1024]{2,1,0:T(8,128)(2,1)S(1)}, bf16[16,16,1024]{2,1,0:T(8,128)(2,1)S(1)}) fusion(bf16[16,16,1024]{2,1,0:T(8,128)(2,1)} %bitcast.128, bf16[1024,1024]{1,0:T(8,128)(2,1)} %bitcast_select_fusion, bf16[1024,1024]{1,0:T(8,128)(2,1)} %collective-permute-done.10, pred[]{:T(512)S(6)} %eq.58), kind=kOutput, calls=%fused_computation.45 | convolution fusion | flops 538968064 | bytes 5767169 | tf_op jit(solution)/shard_map/dot_general | solution.py:139
  102.9 3.0 %constant_dynamic-update-slice_fusion.1 = (bf16[16,48,80]{1,2,0:T(8,128)(2,1)S(1)}, f32[16,48,16]{1,2,0:T(8,128)S(1)}) fusion(bf16[16,48,80]{1,2,0:T(8,128)(2,1)S(1)} %copy-done.14, f32[16,48,16]{1,0,2:T(8,128)S(1)} %copy-done.11, f32[16,48,32]{1,2,0:T(8,128)S(1)} %fusion.22, f32[16,16]{1,0:T(8,128)S(1)} %get-tuple-element.17), kind=kOutput, calls=%fused_computation.82 | output fusion | flops 172335 | bytes 999424 | tf_op jit(solution)/shard_map/sub | solution.py:146
  115.3 4.2 %all-to-all-start.2 = ((f32[8,9,32,128]{3,2,1,0:T(8,128)}), f32[8,9,32,128]{3,2,1,0:T(8,128)}, u32[]{:S(2)}, u32[]{:S(2)}) async-start(f32[8,9,32,128]{3,2,1,0:T(8,128)} %select_select_fusion), calls=%async_computation.2 | async-start | bytes 2359296 | tf_op jit(solution)/shard_map/all_to_all | solution.py:164
  122.5 2.9 %copy.67 = bf16[1024,1024]{1,0:T(8,128)(2,1)S(1)} copy(bf16[1024,1024]{0,1:T(8,128)(2,1)} %fusion.32) | data formatting | bytes 4194304 | tf_op jit(solution)/shard_map/dot_general | solution.py:121
  125.4 3.2 %select_reduce_fusion = bf16[16,16,64]{2,1,0:T(8,128)(2,1)} fusion(pred[16,16]{0,1:T(8,128)(4,1)S(1)} %iota_compare_fusion.1, bf16[2,16,16,1024,1]{3,2,4,1,0:T(8,128)(2,1)S(1)} %bitcast.126, bf16[16,64,1024,1,1]{2,1,0,4,3:T(8,128)(2,1)S(1)} %bitcast.124), kind=kOutput, calls=%fused_computation.6 | convolution fusion | flops 1074774016 | bytes 3178752 | tf_op jit(solution)/shard_map/dot_general | solution.py:121
  129.6 7.3 %all-to-all-done.2 = f32[8,9,32,128]{3,2,1,0:T(8,128)} async-done(((f32[8,9,32,128]{3,2,1,0:T(8,128)}), f32[8,9,32,128]{3,2,1,0:T(8,128)}, u32[]{:S(2)}, u32[]{:S(2)}) %all-to-all-start.2) | async-done | bytes 1179680 | tf_op jit(solution)/shard_map/all_to_all | solution.py:164
  139.1 5.8 %all-to-all-start.3 = ((f32[32,9,128]{2,1,0:T(8,128)}), f32[32,9,128]{2,1,0:T(8,128)S(1)}, u32[]{:S(2)}, u32[]{:S(2)}) async-start(f32[32,9,128]{2,1,0:T(8,128)} %copy.71), calls=%async_computation.3 | async-start | bytes 524288 | tf_op jit(solution)/shard_map/all_to_all | solution.py:165
  144.9 2.6 %convolution_convert_fusion.1 = bf16[16,1024]{1,0:T(8,128)(2,1)} fusion(bf16[16,1024]{1,0:T(8,128)(2,1)S(1)} %convert_element_type.104, bf16[1024,1024]{1,0:T(8,128)(2,1)} %collective-permute-done.10, bf16[1024,1024]{1,0:T(8,128)(2,1)} %bitcast_select_fusion, pred[]{:T(512)S(6)} %eq.58), kind=kOutput, calls=%fused_computation.38 | convolution fusion | flops 34619392 | bytes 4259841 | tf_op jit(solution)/shard_map/dot_general | solution.py:129
  147.5 9.4 %all-to-all-done.3 = f32[32,9,128]{2,1,0:T(8,128)S(1)} async-done(((f32[32,9,128]{2,1,0:T(8,128)}), f32[32,9,128]{2,1,0:T(8,128)S(1)}, u32[]{:S(2)}, u32[]{:S(2)}) %all-to-all-start.3) | async-done | bytes 147488 | tf_op jit(solution)/shard_map/all_to_all | solution.py:165
  (130 shorter events, 48.8 us)
Async XLA Ops:
  0.6 74.1 %copy-start = (bf16[48,4,1024]{2,1,0:T(4,128)(2,1)S(1)}, bf16[48,4,1024]{2,1,0:T(4,128)(2,1)}, u32[]{:S(2)}) copy-start(bf16[48,4,1024]{2,1,0:T(4,128)(2,1)} %param.11) | copy-start | bytes 1179652
  0.7 31.8 %copy-start.19 = (s32[72]{0:T(128)S(1)}, s32[72]{0:T(128)}, u32[]{:S(2)}) copy-start(s32[72]{0:T(128)} %param.10) | copy-start | bytes 868
  1.6 11.0 %collective-permute-start = (bf16[32,1024]{1,0:T(8,128)(2,1)S(1)}, bf16[32,1024]{1,0:T(8,128)(2,1)S(1)}, u32[]{:S(2)}, u32[]{:S(2)}) collective-permute-start(bf16[32,1024]{1,0:T(8,128)(2,1)S(1)} %get-tuple-element.9), channel_id=1, source_target_pairs={{0,1},{1,2},{2,3},{3,4},{4,5},{5,6},{6,7},{7,0},{8,9},{9,10},{10,1... | collective-permute-start | bytes 196616 | tf_op jit(solution)/shard_map/ppermute | solution.py:48
  3.6 11.0 %collective-permute-start.4 = (bf16[32,1024]{1,0:T(8,128)(2,1)S(1)}, bf16[32,1024]{1,0:T(8,128)(2,1)S(1)}, u32[]{:S(2)}, u32[]{:S(2)}) collective-permute-start(bf16[32,1024]{1,0:T(8,128)(2,1)S(1)} %get-tuple-element.9), channel_id=1, source_target_pairs={{0,7},{1,0},{2,1},{3,2},{4,3},{5,4},{6,5},{7,6},{8,15},{9,8},{10,9... | collective-permute-start | bytes 196616 | tf_op jit(solution)/shard_map/ppermute | solution.py:51
  5.3 58.5 %all-to-all-start.1 = ((bf16[8,2,288]{2,1,0:T(2,128)(2,1)}), bf16[8,2,288]{2,1,0:T(2,128)(2,1)S(1)}, u32[]{:S(2)}, u32[]{:S(2)}) async-start(bf16[8,2,288]{2,1,0:T(2,128)(2,1)} %reshape.267), calls=%async_computation.1 | async-start | bytes 24576 | tf_op jit(solution)/shard_map/all_to_all | solution.py:104
  12.6 6.9 %collective-permute-start.1 = (bf16[32,1024]{1,0:T(8,128)(2,1)S(1)}, bf16[32,1024]{1,0:T(8,128)(2,1)S(1)}, u32[]{:S(2)}, u32[]{:S(2)}) collective-permute-start(bf16[32,1024]{1,0:T(8,128)(2,1)S(1)} %collective-permute-done), channel_id=1, source_target_pairs={{0,1},{1,2},{2,3},{3,4},{4,5},{5,6},{6,7},{7,0},{8,9},{9,10},{10,1... | collective-permute-start | bytes 196616 | tf_op jit(solution)/shard_map/ppermute | solution.py:48
  14.6 5.6 %collective-permute-start.5 = (bf16[32,1024]{1,0:T(8,128)(2,1)S(1)}, bf16[32,1024]{1,0:T(8,128)(2,1)S(1)}, u32[]{:S(2)}, u32[]{:S(2)}) collective-permute-start(bf16[32,1024]{1,0:T(8,128)(2,1)S(1)} %collective-permute-done.4), channel_id=1, source_target_pairs={{0,7},{1,0},{2,1},{3,2},{4,3},{5,4},{6,5},{7,6},{8,15},{9,8},{10,9... | collective-permute-start | bytes 196616 | tf_op jit(solution)/shard_map/ppermute | solution.py:51
  19.4 5.2 %collective-permute-start.2 = (bf16[32,1024]{1,0:T(8,128)(2,1)S(1)}, bf16[32,1024]{1,0:T(8,128)(2,1)S(1)}, u32[]{:S(2)}, u32[]{:S(2)}) collective-permute-start(bf16[32,1024]{1,0:T(8,128)(2,1)S(1)} %collective-permute-done.1), channel_id=1, source_target_pairs={{0,1},{1,2},{2,3},{3,4},{4,5},{5,6},{6,7},{7,0},{8,9},{9,10},{10,1... | collective-permute-start | bytes 196616 | tf_op jit(solution)/shard_map/ppermute | solution.py:48
  20.2 10.0 %collective-permute-start.6 = (bf16[32,1024]{1,0:T(8,128)(2,1)S(1)}, bf16[32,1024]{1,0:T(8,128)(2,1)S(1)}, u32[]{:S(2)}, u32[]{:S(2)}) collective-permute-start(bf16[32,1024]{1,0:T(8,128)(2,1)S(1)} %collective-permute-done.5), channel_id=1, source_target_pairs={{0,7},{1,0},{2,1},{3,2},{4,3},{5,4},{6,5},{7,6},{8,15},{9,8},{10,9... | collective-permute-start | bytes 196616 | tf_op jit(solution)/shard_map/ppermute | solution.py:51
  24.6 5.5 %collective-permute-start.3 = (bf16[32,1024]{1,0:T(8,128)(2,1)S(1)}, bf16[32,1024]{1,0:T(8,128)(2,1)S(1)}, u32[]{:S(2)}, u32[]{:S(2)}) collective-permute-start(bf16[32,1024]{1,0:T(8,128)(2,1)S(1)} %collective-permute-done.2), channel_id=1, source_target_pairs={{0,1},{1,2},{2,3},{3,4},{4,5},{5,6},{6,7},{7,0},{8,9},{9,10},{10,1... | collective-permute-start | bytes 196616 | tf_op jit(solution)/shard_map/ppermute | solution.py:48
  30.9 12.7 %collective-permute-start.7 = (bf16[8,32,1024]{2,1,0:T(8,128)(2,1)S(1)}, bf16[8,32,1024]{2,1,0:T(8,128)(2,1)S(1)}, u32[]{:S(2)}, u32[]{:S(2)}) collective-permute-start(bf16[8,32,1024]{2,1,0:T(8,128)(2,1)S(1)} %broadcast_select_fusion.6), channel_id=1, source_target_pairs={{0,8},{1,9},{2,10},{3,11},{4,12},{5,13},{6,14},{7,15},{8,16},{9,17... | collective-permute-start | bytes 1572872 | tf_op jit(solution)/shard_map/ppermute | solution.py:48
  32.5 42.2 %copy-start.17 = (pred[48]{0:T(512)(128)(4,1)}, pred[48]{0:T(512)(128)(4,1)S(1)}, u32[]{:S(2)}) copy-start(pred[48]{0:T(512)(128)(4,1)S(1)} %compare_and_fusion.3) | copy-start | bytes 148
  32.5 12.4 %collective-permute-start.9 = (bf16[8,32,1024]{2,1,0:T(8,128)(2,1)S(1)}, bf16[8,32,1024]{2,1,0:T(8,128)(2,1)S(1)}, u32[]{:S(2)}, u32[]{:S(2)}) collective-permute-start(bf16[8,32,1024]{2,1,0:T(8,128)(2,1)S(1)} %broadcast_select_fusion.6), channel_id=1, source_target_pairs={{0,24},{1,25},{2,26},{3,27},{4,28},{5,29},{6,30},{7,31},{8,0},{9,1... | collective-permute-start | bytes 1572872 | tf_op jit(solution)/shard_map/ppermute | solution.py:51
  43.6 11.8 %collective-permute-start.8 = (bf16[8,32,1024]{2,1,0:T(8,128)(2,1)S(1)}, bf16[8,32,1024]{2,1,0:T(8,128)(2,1)S(1)}, u32[]{:S(2)}, u32[]{:S(2)}) collective-permute-start(bf16[8,32,1024]{2,1,0:T(8,128)(2,1)S(1)} %collective-permute-done.7), channel_id=1, source_target_pairs={{0,8},{1,9},{2,10},{3,11},{4,12},{5,13},{6,14},{7,15},{8,16},{9,17... | collective-permute-start | bytes 1572872 | tf_op jit(solution)/shard_map/ppermute | solution.py:48
  61.1 32.4 %collective-permute-start.10 = (bf16[1024,1024]{1,0:T(8,128)(2,1)}, bf16[1024,1024]{1,0:T(8,128)(2,1)}, u32[]{:S(2)}, u32[]{:S(2)}) collective-permute-start(bf16[1024,1024]{1,0:T(8,128)(2,1)} %bitcast_select_fusion), channel_id=1, source_target_pairs={{0,32},{32,0},{64,96},{96,64},{128,160},{160,128},{192,224},{224,1... | collective-permute-start | bytes 6291464 | tf_op jit(solution)/shard_map/ppermute | solution.py:101
  63.8 18.7 %all-to-all-start = ((f32[32,1,512]{2,1,0:T(1,128)}), f32[32,1,512]{2,1,0:T(1,128)S(1)}, u32[]{:S(2)}, u32[]{:S(2)}) async-start(f32[32,1,512]{2,1,0:T(1,128)} %reshape.269), calls=%async_computation | async-start | bytes 131072 | tf_op jit(solution)/shard_map/all_to_all | solution.py:96
  84.2 6.6 %copy-start.1 = (bf16[48,16,1024]{2,1,0:T(8,128)(2,1)S(1)}, bf16[48,16,1024]{2,1,0:T(8,128)(2,1)}, u32[]{:S(2)}) copy-start(bf16[48,16,1024]{2,1,0:T(8,128)(2,1)} %get-tuple-element.13) | copy-start | bytes 4718596
  89.2 4.3 %copy-start.10 = (f32[16,48,16]{1,0,2:T(8,128)}, f32[16,48,16]{1,0,2:T(8,128)S(1)}, u32[]{:S(2)}) copy-start(f32[16,48,16]{1,0,2:T(8,128)S(1)} %get-tuple-element.18) | copy-start | bytes 147460
  89.2 4.3 %copy-start.20 = (bf16[16,1024]{1,0:T(8,128)(2,1)S(1)}, bf16[16,1024]{1,0:T(8,128)(2,1)}, u32[]{:S(2)}) copy-start(bf16[16,1024]{1,0:T(8,128)(2,1)} %param.17) | copy-start | bytes 98308
  101.7 4.2 %copy-start.7 = (bf16[48,1024]{1,0:T(8,128)(2,1)S(1)}, bf16[48,1024]{1,0:T(8,128)(2,1)}, u32[]{:S(2)}) copy-start(bf16[48,1024]{1,0:T(8,128)(2,1)} %pad_maximum_fusion.2) | copy-start | bytes 294916
  114.0 5.5 %copy-start.4 = (bf16[16,16,1024]{2,1,0:T(8,128)(2,1)S(1)}, bf16[16,16,1024]{2,1,0:T(8,128)(2,1)}, u32[]{:S(2)}) copy-start(bf16[16,16,1024]{2,1,0:T(8,128)(2,1)} %get-tuple-element.10) | copy-start | bytes 1572868
  114.1 5.5 %copy-start.5 = (bf16[16,16,1024]{2,1,0:T(8,128)(2,1)S(1)}, bf16[16,16,1024]{2,1,0:T(8,128)(2,1)}, u32[]{:S(2)}) copy-start(bf16[16,16,1024]{2,1,0:T(8,128)(2,1)} %get-tuple-element.11) | copy-start | bytes 1572868
  115.3 21.6 %all-to-all-start.2 = ((f32[8,9,32,128]{3,2,1,0:T(8,128)}), f32[8,9,32,128]{3,2,1,0:T(8,128)}, u32[]{:S(2)}, u32[]{:S(2)}) async-start(f32[8,9,32,128]{3,2,1,0:T(8,128)} %select_select_fusion), calls=%async_computation.2 | async-start | bytes 2359296 | tf_op jit(solution)/shard_map/all_to_all | solution.py:164
  139.1 17.8 %all-to-all-start.3 = ((f32[32,9,128]{2,1,0:T(8,128)}), f32[32,9,128]{2,1,0:T(8,128)S(1)}, u32[]{:S(2)}, u32[]{:S(2)}) async-start(f32[32,9,128]{2,1,0:T(8,128)} %copy.71), calls=%async_computation.3 | async-start | bytes 524288 | tf_op jit(solution)/shard_map/all_to_all | solution.py:165
  (12 other events, 23.5 us)
where the time goes:
time: 158 us
  waiting for transfers between devices  51.2 us (32%)
  starting transfers between devices  37.3 us (24%)
  matrix products  26 us (16%)
  local copies, waits for them, and re-layouts  24 us (15%)
  other arithmetic  17.8 us (11%)
    ppermute x6, waiting for transfers between devices, ring_steps(): forward = lax.ppermute(forward, 'tok', perm_of(1))  29.9 us
    dot_general x6, matrix products, ein(): return jnp.einsum(spec, a, b, preferred_element_type=f32)  13.3 us
    all_to_all x1, starting transfers between devices, body(): lax.all_to_all(wq_copies, 'tok', 0, 0, tiled=True).reshape(n_tok * rows, H)  9.54 us
    all_to_all x1, waiting for transfers between devices, body(): lax.all_to_all(by_var.transpose(1, 0, 2), 'tok', 0, 0, tiled=True)  9.36 us
    all_to_all x1, waiting for transfers between devices, body(): by_var = lax.all_to_all(blocks, 'var', 0, 0, tiled=True).sum(axis=0)  7.33 us
    unnamed x57, local copies, waits for them, and re-layouts  6.9 us
    ppermute x6, starting transfers between devices, ring_steps(): forward = lax.ppermute(forward, 'tok', perm_of(1))  6.75 us
    ppermute x4, starting transfers between devices, ring_steps(): backward = lax.ppermute(backward, 'tok', perm_of(-1))  6.48 us
  transfers between devices with their start and end apart: 15, of which 9 were waited for; matrix products, arithmetic and copies ran while one was open for 26% of the time, Pallas kernels for 0%

commit v1 on v0

--- a/solution.py
+++ b/solution.py
@@ -11,6 +11,22 @@
 inv_sqrt_two_pi = 1.0 / math.sqrt(2.0 * math.pi)
 f32 = jnp.float32
 bf16 = jnp.bfloat16
+
+
+def exchange_in_pairs(value, axis, split, join):
+    ways, here = (lax.axis_size(axis), lax.axis_index(axis))
+    width = value.shape[split] // ways
+    lengths = list(value.shape)
+    lengths[split] = width
+    height = lengths[join]
+    lengths[join] = height * ways
+    full = jnp.zeros(lengths, value.dtype)
+    for mask in range(ways):
+        part = lax.dynamic_slice_in_dim(value, (here ^ mask) * width, width, axis=split)
+        if mask:
+            part = lax.ppermute(part, axis, [(d, d ^ mask) for d in range(ways)])
+        full = lax.dynamic_update_slice_in_dim(full, part, (here ^ mask) * height, axis=join)
+    return full
 
 
 def gelu_exact(inputs):
@@ -101,7 +117,7 @@
     other = lax.ppermute(gathered, "var", [(i, i ^ 1) for i in range(n_var)])
     value_matrix = jnp.where(core == 0, gathered, other)
     out_matrix = jnp.where(core == 0, other, gathered)
-    slot_pixels = lax.all_to_all(patches, "var", 2, 0, tiled=True)
+    slot_pixels = exchange_in_pairs(patches, "var", 2, 0)
     live_slot = live_index(slot_var, var_total)
     pixels = jnp.take(slot_pixels, live_slot, axis=0)
     pre_act = ein("vpt,vpd->vtd", pixels, patch_weight) + var_embed.astype(f32)[:, None, :]

time: 158 us -> 157 us (level)
  waiting for transfers between devices: 51.2 us -> 39.1 us
  starting transfers between devices: 37.3 us -> 48.5 us
    ppermute x6, waiting for transfers between devices: 29.9 us -> 11.3 us  [ring_steps(): forward = lax.ppermute(forward, 'tok', perm_of(1))]
    ppermute x4, waiting for transfers between devices: 0.55 us -> 11.1 us  [ring_steps(): backward = lax.ppermute(backward, 'tok', perm_of(-1))]
    ppermute x0 -> x7, starting transfers between devices: none -> 8.41 us  [exchange_in_pairs(): part = lax.ppermute(part, axis, [(d, d ^ mask) for d in range(ways)])]
    all_to_all x1 -> x0, starting transfers between devices: 4.47 us -> none  [body(): slot_pixels = lax.all_to_all(patches, 'var', 2, 0, tiled=True)]
    all_to_all x1, waiting for transfers between devices: 4 us -> 0.01 us  [body(): lax.all_to_all(wq_copies, 'tok', 0, 0, tiled=True).reshape(n_tok * rows, H)]
    all_to_all x1, starting transfers between devices: 5.78 us -> 9.39 us  [body(): lax.all_to_all(by_var.transpose(1, 0, 2), 'tok', 0, 0, tiled=True)]
    all_to_all x1, starting transfers between devices: 9.54 us -> 12.4 us  [body(): lax.all_to_all(wq_copies, 'tok', 0, 0, tiled=True).reshape(n_tok * rows, H)]
    unnamed x57 -> x52, local copies, waits for them, and re-layouts: 6.9 us -> 4.93 us
  transfers between devices with their start and end apart: 15 -> 21, of which waited for: 9 -> 9; matrix products, arithmetic and copies ran while one was open for 26% -> 26% of each run, Pallas kernels for 0% -> 0%
where the time goes in v1:
time: 157 us; the launch traced here: 156 us
  starting transfers between devices  48.5 us (31%)
  waiting for transfers between devices  39.1 us (25%)
  matrix products  26.1 us (17%)
  local copies, waits for them, and re-layouts  23 us (15%)
  other arithmetic  18.5 us (12%)
    dot_general x6, matrix products, ein(): return jnp.einsum(spec, a, b, preferred_element_type=f32)  13.4 us
    all_to_all x1, starting transfers between devices, body(): lax.all_to_all(wq_copies, 'tok', 0, 0, tiled=True).reshape(n_tok * rows, H)  12.4 us
    ppermute x6, waiting for transfers between devices, ring_steps(): forward = lax.ppermute(forward, 'tok', perm_of(1))  11.3 us
    ppermute x4, waiting for transfers between devices, ring_steps(): backward = lax.ppermute(backward, 'tok', perm_of(-1))  11.1 us
    all_to_all x1, starting transfers between devices, body(): lax.all_to_all(by_var.transpose(1, 0, 2), 'tok', 0, 0, tiled=True)  9.39 us
    all_to_all x1, waiting for transfers between devices, body(): lax.all_to_all(by_var.transpose(1, 0, 2), 'tok', 0, 0, tiled=True)  9.36 us
    ppermute x6, starting transfers between devices, ring_steps(): forward = lax.ppermute(forward, 'tok', perm_of(1))  8.58 us
    ppermute x7, starting transfers between devices, exchange_in_pairs(): part = lax.ppermute(part, axis, [(d, d ^ mask) for d in range(ways)])  8.41 us
  transfers between devices with their start and end apart: 21, of which 9 were waited for; matrix products, arithmetic and copies ran while one was open for 26% of the time, Pallas kernels for 0%

profile of v1, /device:TPU:32, one launch (start us, length us, event | category | flops | bytes accessed | tf_op | source)
XLA Modules:
  0.0 156.5 jit_solution(5017771163051278418)
XLA Ops:
  9.6 12.4 %all-to-all-start = ((f32[32,1,512]{2,1,0:T(1,128)}), f32[32,1,512]{2,1,0:T(1,128)S(1)}, u32[]{:S(2)}, u32[]{:S(2)}) async-start(f32[32,1,512]{2,1,0:T(1,128)} %reshape.267), calls=%async_computation | async-start | bytes 131072 | tf_op jit(solution)/shard_map/all_to_all | solution.py:112
  26.4 2.1 %collective-permute-done.8 = bf16[32,1024]{1,0:T(8,128)(2,1)S(1)} collective-permute-done((bf16[32,1024]{1,0:T(8,128)(2,1)S(1)}, bf16[32,1024]{1,0:T(8,128)(2,1)S(1)}, u32[]{:S(2)}, u32[]{:S(2)}) %collective-permute-start.8) | collective-permute-done | bytes 65568 | tf_op jit(solution)/shard_map/ppermute | solution.py:64
  30.0 2.8 %collective-permute-done.9 = bf16[32,1024]{1,0:T(8,128)(2,1)S(1)} collective-permute-done((bf16[32,1024]{1,0:T(8,128)(2,1)S(1)}, bf16[32,1024]{1,0:T(8,128)(2,1)S(1)}, u32[]{:S(2)}, u32[]{:S(2)}) %collective-permute-start.9) | collective-permute-done | bytes 65568 | tf_op jit(solution)/shard_map/ppermute | solution.py:64
  34.3 3.3 %collective-permute-start.3 = (bf16[9,4,16]{2,1,0:T(4,128)(2,1)S(1)}, bf16[9,4,16]{2,1,0:T(4,128)(2,1)S(1)}, u32[]{:S(2)}, u32[]{:S(2)}) collective-permute-start(bf16[9,4,16]{2,1,0:T(4,128)(2,1)S(1)} %get-tuple-element.18), channel_id=1, source_target_pairs={{0,128},{32,160},{64,192},{96,224},{128,0},{160,32},{192,64},{224,... | collective-permute-start | bytes 3464 | tf_op jit(solution)/shard_map/ppermute | solution.py:27
  37.8 3.2 %collective-permute-start.13 = (bf16[32,1024]{1,0:T(8,128)(2,1)S(1)}, bf16[32,1024]{1,0:T(8,128)(2,1)S(1)}, u32[]{:S(2)}, u32[]{:S(2)}) collective-permute-start(bf16[32,1024]{1,0:T(8,128)(2,1)S(1)} %collective-permute-done.12), channel_id=1, source_target_pairs={{0,7},{1,0},{2,1},{3,2},{4,3},{5,4},{6,5},{7,6},{8,15},{9,8},{10,9... | collective-permute-start | bytes 196616 | tf_op jit(solution)/shard_map/ppermute | solution.py:67
  47.2 3.1 %collective-permute-start.5 = (bf16[9,4,16]{2,1,0:T(4,128)(2,1)S(1)}, bf16[9,4,16]{2,1,0:T(4,128)(2,1)S(1)}, u32[]{:S(2)}, u32[]{:S(2)}) collective-permute-start(bf16[9,4,16]{2,1,0:T(4,128)(2,1)S(1)} %get-tuple-element.23), channel_id=1, source_target_pairs={{0,192},{32,224},{64,128},{96,160},{128,64},{160,96},{192,0},{224,... | collective-permute-start | bytes 3464 | tf_op jit(solution)/shard_map/ppermute | solution.py:27
  51.8 3.5 %collective-permute-done.14 = bf16[8,32,1024]{2,1,0:T(8,128)(2,1)S(1)} collective-permute-done((bf16[8,32,1024]{2,1,0:T(8,128)(2,1)S(1)}, bf16[8,32,1024]{2,1,0:T(8,128)(2,1)S(1)}, u32[]{:S(2)}, u32[]{:S(2)}) %collective-permute-start.14) | collective-permute-done | bytes 524320 | tf_op jit(solution)/shard_map/ppermute | solution.py:64
  55.9 9.1 %collective-permute-done.16 = bf16[8,32,1024]{2,1,0:T(8,128)(2,1)S(1)} collective-permute-done((bf16[8,32,1024]{2,1,0:T(8,128)(2,1)S(1)}, bf16[8,32,1024]{2,1,0:T(8,128)(2,1)S(1)}, u32[]{:S(2)}, u32[]{:S(2)}) %collective-permute-start.16) | collective-permute-done | bytes 524320 | tf_op jit(solution)/shard_map/ppermute | solution.py:67
  65.1 2.6 %collective-permute-done.15 = bf16[8,32,1024]{2,1,0:T(8,128)(2,1)S(1)} collective-permute-done((bf16[8,32,1024]{2,1,0:T(8,128)(2,1)S(1)}, bf16[8,32,1024]{2,1,0:T(8,128)(2,1)S(1)}, u32[]{:S(2)}, u32[]{:S(2)}) %collective-permute-start.15) | collective-permute-done | bytes 524320 | tf_op jit(solution)/shard_map/ppermute | solution.py:64
  69.3 2.3 %gather_fusion.2 = bf16[4,8,32,1024]{3,2,1,0:T(8,128)(2,1)S(1)} fusion(bf16[4,8,32,1024]{3,2,1,0:T(8,128)(2,1)} %pad_maximum_fusion, s32[1024]{0:T(1024)S(1)} %pad_clamp_fusion.1), kind=kCustom, calls=%fused_computation.2 | custom fusion | bytes 4194320 | tf_op jit(solution)/shard_map/jit(_take)/gather | solution.py:85
  74.0 3.8 %fusion.4 = (f32[48,16,1024]{2,1,0:T(8,128)}, bf16[48,16,1024]{2,1,0:T(8,128)(2,1)}) fusion(f32[48,1024]{1,0:T(8,128)S(1)} %convert_element_type.95, bf16[48,4,1024]{2,1,0:T(4,128)(2,1)S(1)} %copy-done, bf16[48,4,16]{2,1,0:T(4,128)(2,1)S(1)} %gather_fusion, pred[48]{0:T(512)(128)(4,1)S(1)} %compare_and_fusion.3), kind=kOutput, calls=%fused_computation.10 | convolution fusion | flops 15731712 | bytes 5314608 | tf_op jit(solution)/shard_map/vpt,vpd->vtd/dot_general | solution.py:57
  79.5 2.5 %fusion.30 = f32[16,48,16]{1,0,2:T(8,128)S(1)} fusion(bf16[48,16,1024]{2,1,0:T(8,128)(2,1)} %get-tuple-element.13, f32[1024,16]{0,1:T(8,128)S(1)} %reshape.224), kind=kOutput, calls=%fused_computation.52 | convolution fusion | flops 25182208 | bytes 1687552 | tf_op jit(solution)/shard_map/vtd,dh->tvh/dot_general | solution.py:57
  82.0 2.5 %bitcast_reduce_fusion = (f32[16,16]{1,0:T(8,128)S(1)}, f32[16,48,16]{1,0,2:T(8,128)S(1)}) fusion(f32[16,48,16]{1,0,2:T(8,128)S(1)} %fusion.30, bf16[48,16,1024]{2,1,0:T(8,128)(2,1)} %get-tuple-element.13, f32[1024,16]{0,1:T(8,128)S(1)} %reshape.224), kind=kOutput, calls=%fused_computation.60 | convolution fusion | flops 25280256 | bytes 1737728 | tf_op jit(solution)/shard_map/vtd,dh->tvh/dot_general | solution.py:57
  86.1 2.7 %subtract_convert_fusion.1 = (bf16[16,16,1024]{2,1,0:T(8,128)(2,1)}, bf16[16,16,1024]{2,1,0:T(8,128)(2,1)}) fusion(bf16[16,48,16]{1,2,0:T(8,128)(2,1)S(1)} %get-tuple-element.7, bf16[48,16,1024]{2,1,0:T(8,128)(2,1)S(1)} %copy-done.1), kind=kOutput, calls=%fused_computation.46 | convolution fusion | flops 26214400 | bytes 2646016 | tf_op jit(solution)/shard_map/tvh,vtd->thd/dot_general | solution.py:57
  88.9 2.2 %fusion.21 = bf16[16,1024]{1,0:T(8,128)(2,1)S(1)} fusion(bf16[1024,16]{0,1:T(8,128)(2,1)S(1)} %bitcast.126, bf16[1024,1024]{1,0:T(8,128)(2,1)} %collective-permute-done.17, bf16[1024,1024]{1,0:T(8,128)(2,1)} %bitcast_select_fusion, pred[]{:T(512)S(6)} %eq.58), kind=kOutput, calls=%fused_computation.39 | convolution fusion | flops 34619392 | bytes 4259841 | tf_op jit(solution)/shard_map/dot_general | solution.py:148
  94.4 2.6 %subtract_convert_fusion = (bf16[16,16,1024]{2,1,0:T(8,128)(2,1)S(1)}, bf16[16,16,1024]{2,1,0:T(8,128)(2,1)S(1)}) fusion(bf16[16,16,1024]{2,1,0:T(8,128)(2,1)} %bitcast.121, bf16[1024,1024]{1,0:T(8,128)(2,1)} %bitcast_select_fusion, bf16[1024,1024]{1,0:T(8,128)(2,1)} %collective-permute-done.17, pred[]{:T(512)S(6)} %eq.58), kind=kOutput, calls=%fused_computation.45 | convolution fusion | flops 538968064 | bytes 5767169 | tf_op jit(solution)/shard_map/dot_general | solution.py:155
  98.2 3.0 %constant_dynamic-update-slice_fusion.1 = (bf16[16,48,80]{1,2,0:T(8,128)(2,1)S(1)}, f32[16,48,16]{1,2,0:T(8,128)S(1)}) fusion(bf16[16,48,80]{1,2,0:T(8,128)(2,1)S(1)} %copy-done.14, f32[16,48,16]{1,0,2:T(8,128)S(1)} %copy-done.11, f32[16,48,32]{1,2,0:T(8,128)S(1)} %fusion.22, f32[16,16]{1,0:T(8,128)S(1)} %get-tuple-element.25), kind=kOutput, calls=%fused_computation.81 | output fusion | flops 172335 | bytes 999424 | tf_op jit(solution)/shard_map/sub | solution.py:162
  110.7 4.2 %all-to-all-start.1 = ((f32[8,9,32,128]{3,2,1,0:T(8,128)}), f32[8,9,32,128]{3,2,1,0:T(8,128)}, u32[]{:S(2)}, u32[]{:S(2)}) async-start(f32[8,9,32,128]{3,2,1,0:T(8,128)} %select_select_fusion), calls=%async_computation.1 | async-start | bytes 2359296 | tf_op jit(solution)/shard_map/all_to_all | solution.py:180
  117.8 2.9 %copy.53 = bf16[1024,1024]{1,0:T(8,128)(2,1)S(1)} copy(bf16[1024,1024]{0,1:T(8,128)(2,1)} %fusion.32) | data formatting | bytes 4194304 | tf_op jit(solution)/shard_map/dot_general | solution.py:137
  120.8 3.2 %select_reduce_fusion = bf16[16,16,64]{2,1,0:T(8,128)(2,1)} fusion(pred[16,16]{0,1:T(8,128)(4,1)S(1)} %iota_compare_fusion.1, bf16[2,16,16,1024,1]{3,2,4,1,0:T(8,128)(2,1)S(1)} %bitcast.119, bf16[16,64,1024,1,1]{2,1,0,4,3:T(8,128)(2,1)S(1)} %bitcast.117), kind=kOutput, calls=%fused_computation.6 | convolution fusion | flops 1074774016 | bytes 3178752 | tf_op jit(solution)/shard_map/dot_general | solution.py:137
  125.0 7.3 %all-to-all-done.1 = f32[8,9,32,128]{3,2,1,0:T(8,128)} async-done(((f32[8,9,32,128]{3,2,1,0:T(8,128)}), f32[8,9,32,128]{3,2,1,0:T(8,128)}, u32[]{:S(2)}, u32[]{:S(2)}) %all-to-all-start.1) | async-done | bytes 1179680 | tf_op jit(solution)/shard_map/all_to_all | solution.py:180
  134.4 9.4 %all-to-all-start.2 = ((f32[32,9,128]{2,1,0:T(8,128)}), f32[32,9,128]{2,1,0:T(8,128)S(1)}, u32[]{:S(2)}, u32[]{:S(2)}) async-start(f32[32,9,128]{2,1,0:T(8,128)} %copy.57), calls=%async_computation.2 | async-start | bytes 524288 | tf_op jit(solution)/shard_map/all_to_all | solution.py:181
  143.8 2.6 %convolution_convert_fusion.1 = bf16[16,1024]{1,0:T(8,128)(2,1)} fusion(bf16[16,1024]{1,0:T(8,128)(2,1)S(1)} %convert_element_type.104, bf16[1024,1024]{1,0:T(8,128)(2,1)} %collective-permute-done.17, bf16[1024,1024]{1,0:T(8,128)(2,1)} %bitcast_select_fusion, pred[]{:T(512)S(6)} %eq.58), kind=kOutput, calls=%fused_computation.38 | convolution fusion | flops 34619392 | bytes 4259841 | tf_op jit(solution)/shard_map/dot_general | solution.py:145
  146.5 9.4 %all-to-all-done.2 = f32[32,9,128]{2,1,0:T(8,128)S(1)} async-done(((f32[32,9,128]{2,1,0:T(8,128)}), f32[32,9,128]{2,1,0:T(8,128)S(1)}, u32[]{:S(2)}, u32[]{:S(2)}) %all-to-all-start.2) | async-done | bytes 147488 | tf_op jit(solution)/shard_map/all_to_all | solution.py:181
  (144 shorter events, 52.1 us)
Async XLA Ops:
  0.6 73.3 %copy-start = (bf16[48,4,1024]{2,1,0:T(4,128)(2,1)S(1)}, bf16[48,4,1024]{2,1,0:T(4,128)(2,1)}, u32[]{:S(2)}) copy-start(bf16[48,4,1024]{2,1,0:T(4,128)(2,1)} %param.11) | copy-start | bytes 1179652
  1.6 22.6 %collective-permute-start.7 = (bf16[32,1024]{1,0:T(8,128)(2,1)S(1)}, bf16[32,1024]{1,0:T(8,128)(2,1)S(1)}, u32[]{:S(2)}, u32[]{:S(2)}) collective-permute-start(bf16[32,1024]{1,0:T(8,128)(2,1)S(1)} %get-tuple-element.9), channel_id=1, source_target_pairs={{0,1},{1,2},{2,3},{3,4},{4,5},{5,6},{6,7},{7,0},{8,9},{9,10},{10,1... | collective-permute-start | bytes 196616 | tf_op jit(solution)/shard_map/ppermute | solution.py:64
  3.6 22.2 %collective-permute-start.11 = (bf16[32,1024]{1,0:T(8,128)(2,1)S(1)}, bf16[32,1024]{1,0:T(8,128)(2,1)S(1)}, u32[]{:S(2)}, u32[]{:S(2)}) collective-permute-start(bf16[32,1024]{1,0:T(8,128)(2,1)S(1)} %get-tuple-element.9), channel_id=1, source_target_pairs={{0,7},{1,0},{2,1},{3,2},{4,3},{5,4},{6,5},{7,6},{8,15},{9,8},{10,9... | collective-permute-start | bytes 196616 | tf_op jit(solution)/shard_map/ppermute | solution.py:67
  4.8 42.3 %collective-permute-start = (bf16[9,4,16]{2,1,0:T(4,128)(2,1)S(1)}, bf16[9,4,16]{2,1,0:T(4,128)(2,1)S(1)}, u32[]{:S(2)}, u32[]{:S(2)}) collective-permute-start(bf16[9,4,16]{2,1,0:T(4,128)(2,1)S(1)} %get-tuple-element.21), channel_id=1, source_target_pairs={{0,32},{32,0},{64,96},{96,64},{128,160},{160,128},{192,224},{224,1... | collective-permute-start | bytes 3464 | tf_op jit(solution)/shard_map/ppermute | solution.py:27
  4.9 42.2 %collective-permute-start.1 = (bf16[9,4,16]{2,1,0:T(4,128)(2,1)S(1)}, bf16[9,4,16]{2,1,0:T(4,128)(2,1)S(1)}, u32[]{:S(2)}, u32[]{:S(2)}) collective-permute-start(bf16[9,4,16]{2,1,0:T(4,128)(2,1)S(1)} %get-tuple-element.20), channel_id=1, source_target_pairs={{0,64},{32,96},{64,0},{96,32},{128,192},{160,224},{192,128},{224,1... | collective-permute-start | bytes 3464 | tf_op jit(solution)/shard_map/ppermute | solution.py:27
  6.6 43.7 %collective-permute-start.2 = (bf16[9,4,16]{2,1,0:T(4,128)(2,1)S(1)}, bf16[9,4,16]{2,1,0:T(4,128)(2,1)S(1)}, u32[]{:S(2)}, u32[]{:S(2)}) collective-permute-start(bf16[9,4,16]{2,1,0:T(4,128)(2,1)S(1)} %get-tuple-element.19), channel_id=1, source_target_pairs={{0,96},{32,64},{64,32},{96,0},{128,224},{160,192},{192,160},{224,1... | collective-permute-start | bytes 3464 | tf_op jit(solution)/shard_map/ppermute | solution.py:27
  7.8 37.9 %copy-start.12 = (bf16[48,1024]{1,0:T(8,128)(2,1)S(1)}, bf16[48,1024]{1,0:T(8,128)(2,1)}, u32[]{:S(2)}) copy-start(bf16[48,1024]{1,0:T(8,128)(2,1)} %param.12) | copy-start | bytes 294916
  9.6 68.2 %all-to-all-start = ((f32[32,1,512]{2,1,0:T(1,128)}), f32[32,1,512]{2,1,0:T(1,128)S(1)}, u32[]{:S(2)}, u32[]{:S(2)}) async-start(f32[32,1,512]{2,1,0:T(1,128)} %reshape.267), calls=%async_computation | async-start | bytes 131072 | tf_op jit(solution)/shard_map/all_to_all | solution.py:112
  24.2 4.3 %collective-permute-start.8 = (bf16[32,1024]{1,0:T(8,128)(2,1)S(1)}, bf16[32,1024]{1,0:T(8,128)(2,1)S(1)}, u32[]{:S(2)}, u32[]{:S(2)}) collective-permute-start(bf16[32,1024]{1,0:T(8,128)(2,1)S(1)} %collective-permute-done.7), channel_id=1, source_target_pairs={{0,1},{1,2},{2,3},{3,4},{4,5},{5,6},{6,7},{7,0},{8,9},{9,10},{10,1... | collective-permute-start | bytes 196616 | tf_op jit(solution)/shard_map/ppermute | solution.py:64
  25.8 8.5 %collective-permute-start.12 = (bf16[32,1024]{1,0:T(8,128)(2,1)S(1)}, bf16[32,1024]{1,0:T(8,128)(2,1)S(1)}, u32[]{:S(2)}, u32[]{:S(2)}) collective-permute-start(bf16[32,1024]{1,0:T(8,128)(2,1)S(1)} %collective-permute-done.11), channel_id=1, source_target_pairs={{0,7},{1,0},{2,1},{3,2},{4,3},{5,4},{6,5},{7,6},{8,15},{9,8},{10,9... | collective-permute-start | bytes 196616 | tf_op jit(solution)/shard_map/ppermute | solution.py:67
  28.6 4.3 %collective-permute-start.9 = (bf16[32,1024]{1,0:T(8,128)(2,1)S(1)}, bf16[32,1024]{1,0:T(8,128)(2,1)S(1)}, u32[]{:S(2)}, u32[]{:S(2)}) collective-permute-start(bf16[32,1024]{1,0:T(8,128)(2,1)S(1)} %collective-permute-done.8), channel_id=1, source_target_pairs={{0,1},{1,2},{2,3},{3,4},{4,5},{5,6},{6,7},{7,0},{8,9},{9,10},{10,1... | collective-permute-start | bytes 196616 | tf_op jit(solution)/shard_map/ppermute | solution.py:64
  32.8 5.0 %collective-permute-start.10 = (bf16[32,1024]{1,0:T(8,128)(2,1)S(1)}, bf16[32,1024]{1,0:T(8,128)(2,1)S(1)}, u32[]{:S(2)}, u32[]{:S(2)}) collective-permute-start(bf16[32,1024]{1,0:T(8,128)(2,1)S(1)} %collective-permute-done.9), channel_id=1, source_target_pairs={{0,1},{1,2},{2,3},{3,4},{4,5},{5,6},{6,7},{7,0},{8,9},{9,10},{10,1... | collective-permute-start | bytes 196616 | tf_op jit(solution)/shard_map/ppermute | solution.py:64
  34.3 21.3 %collective-permute-start.3 = (bf16[9,4,16]{2,1,0:T(4,128)(2,1)S(1)}, bf16[9,4,16]{2,1,0:T(4,128)(2,1)S(1)}, u32[]{:S(2)}, u32[]{:S(2)}) collective-permute-start(bf16[9,4,16]{2,1,0:T(4,128)(2,1)S(1)} %get-tuple-element.18), channel_id=1, source_target_pairs={{0,128},{32,160},{64,192},{96,224},{128,0},{160,32},{192,64},{224,... | collective-permute-start | bytes 3464 | tf_op jit(solution)/shard_map/ppermute | solution.py:27
  37.8 5.1 %collective-permute-start.13 = (bf16[32,1024]{1,0:T(8,128)(2,1)S(1)}, bf16[32,1024]{1,0:T(8,128)(2,1)S(1)}, u32[]{:S(2)}, u32[]{:S(2)}) collective-permute-start(bf16[32,1024]{1,0:T(8,128)(2,1)S(1)} %collective-permute-done.12), channel_id=1, source_target_pairs={{0,7},{1,0},{2,1},{3,2},{4,3},{5,4},{6,5},{7,6},{8,15},{9,8},{10,9... | collective-permute-start | bytes 196616 | tf_op jit(solution)/shard_map/ppermute | solution.py:67
  43.7 11.7 %collective-permute-start.14 = (bf16[8,32,1024]{2,1,0:T(8,128)(2,1)S(1)}, bf16[8,32,1024]{2,1,0:T(8,128)(2,1)S(1)}, u32[]{:S(2)}, u32[]{:S(2)}) collective-permute-start(bf16[8,32,1024]{2,1,0:T(8,128)(2,1)S(1)} %broadcast_select_fusion.6), channel_id=1, source_target_pairs={{0,8},{1,9},{2,10},{3,11},{4,12},{5,13},{6,14},{7,15},{8,16},{9,17... | collective-permute-start | bytes 1572872 | tf_op jit(solution)/shard_map/ppermute | solution.py:64
  45.6 28.4 %copy-start.17 = (pred[48]{0:T(512)(128)(4,1)}, pred[48]{0:T(512)(128)(4,1)S(1)}, u32[]{:S(2)}) copy-start(pred[48]{0:T(512)(128)(4,1)S(1)} %compare_and_fusion.3) | copy-start | bytes 148
  47.1 8.6 %collective-permute-start.4 = (bf16[9,4,16]{2,1,0:T(4,128)(2,1)S(1)}, bf16[9,4,16]{2,1,0:T(4,128)(2,1)S(1)}, u32[]{:S(2)}, u32[]{:S(2)}) collective-permute-start(bf16[9,4,16]{2,1,0:T(4,128)(2,1)S(1)} %get-tuple-element.17), channel_id=1, source_target_pairs={{0,160},{32,128},{64,224},{96,192},{128,32},{160,0},{192,96},{224,... | collective-permute-start | bytes 3464 | tf_op jit(solution)/shard_map/ppermute | solution.py:27
  47.2 26.1 %collective-permute-start.5 = (bf16[9,4,16]{2,1,0:T(4,128)(2,1)S(1)}, bf16[9,4,16]{2,1,0:T(4,128)(2,1)S(1)}, u32[]{:S(2)}, u32[]{:S(2)}) collective-permute-start(bf16[9,4,16]{2,1,0:T(4,128)(2,1)S(1)} %get-tuple-element.23), channel_id=1, source_target_pairs={{0,192},{32,224},{64,128},{96,160},{128,64},{160,96},{192,0},{224,... | collective-permute-start | bytes 3464 | tf_op jit(solution)/shard_map/ppermute | solution.py:27
  50.3 14.8 %collective-permute-start.16 = (bf16[8,32,1024]{2,1,0:T(8,128)(2,1)S(1)}, bf16[8,32,1024]{2,1,0:T(8,128)(2,1)S(1)}, u32[]{:S(2)}, u32[]{:S(2)}) collective-permute-start(bf16[8,32,1024]{2,1,0:T(8,128)(2,1)S(1)} %broadcast_select_fusion.6), channel_id=1, source_target_pairs={{0,24},{1,25},{2,26},{3,27},{4,28},{5,29},{6,30},{7,31},{8,0},{9,1... | collective-permute-start | bytes 1572872 | tf_op jit(solution)/shard_map/ppermute | solution.py:67
  55.4 12.3 %collective-permute-start.15 = (bf16[8,32,1024]{2,1,0:T(8,128)(2,1)S(1)}, bf16[8,32,1024]{2,1,0:T(8,128)(2,1)S(1)}, u32[]{:S(2)}, u32[]{:S(2)}) collective-permute-start(bf16[8,32,1024]{2,1,0:T(8,128)(2,1)S(1)} %collective-permute-done.14), channel_id=1, source_target_pairs={{0,8},{1,9},{2,10},{3,11},{4,12},{5,13},{6,14},{7,15},{8,16},{9,17... | collective-permute-start | bytes 1572872 | tf_op jit(solution)/shard_map/ppermute | solution.py:64
  55.6 17.7 %collective-permute-start.6 = (bf16[9,4,16]{2,1,0:T(4,128)(2,1)S(1)}, bf16[9,4,16]{2,1,0:T(4,128)(2,1)S(1)}, u32[]{:S(2)}, u32[]{:S(2)}) collective-permute-start(bf16[9,4,16]{2,1,0:T(4,128)(2,1)S(1)} %get-tuple-element.16), channel_id=1, source_target_pairs={{0,224},{32,192},{64,160},{96,128},{128,96},{160,64},{192,32},{224... | collective-permute-start | bytes 3464 | tf_op jit(solution)/shard_map/ppermute | solution.py:27
  73.3 15.6 %collective-permute-start.17 = (bf16[1024,1024]{1,0:T(8,128)(2,1)}, bf16[1024,1024]{1,0:T(8,128)(2,1)}, u32[]{:S(2)}, u32[]{:S(2)}) collective-permute-start(bf16[1024,1024]{1,0:T(8,128)(2,1)} %bitcast_select_fusion), channel_id=1, source_target_pairs={{0,32},{32,0},{64,96},{96,64},{128,160},{160,128},{192,224},{224,1... | collective-permute-start | bytes 6291464 | tf_op jit(solution)/shard_map/ppermute | solution.py:117
  110.7 21.6 %all-to-all-start.1 = ((f32[8,9,32,128]{3,2,1,0:T(8,128)}), f32[8,9,32,128]{3,2,1,0:T(8,128)}, u32[]{:S(2)}, u32[]{:S(2)}) async-start(f32[8,9,32,128]{3,2,1,0:T(8,128)} %select_select_fusion), calls=%async_computation.1 | async-start | bytes 2359296 | tf_op jit(solution)/shard_map/all_to_all | solution.py:180
  134.4 21.4 %all-to-all-start.2 = ((f32[32,9,128]{2,1,0:T(8,128)}), f32[32,9,128]{2,1,0:T(8,128)S(1)}, u32[]{:S(2)}, u32[]{:S(2)}) async-start(f32[32,9,128]{2,1,0:T(8,128)} %copy.57), calls=%async_computation.2 | async-start | bytes 524288 | tf_op jit(solution)/shard_map/all_to_all | solution.py:181
  (17 other events, 51.5 us)
